TPU v7x, 128 devices: a whole 4x4x4 slice. The times are simulated.
128 devices in a mesh: wide: 64 (over z, y, x), narrow: 2 (over core).
Axes of the slice: x: 4, y: 4, z: 4, core: 2. Of those that a mesh axis runs over, the one named last changes fastest.
Arguments:
- tokens: bfloat16 [65536, 2048], P('wide', 'narrow'), may hold values from -6 to 6
- attn_gain: bfloat16 [2048], replicated, may hold values from 0.5 to 1.5
- q_weight: bfloat16 [2048, 3072], P('wide', 'narrow'), may hold values from -6 to 6
- kva_weight: bfloat16 [2048, 576], P('wide'), may hold values from -0.125 to 0.125
- kv_gain: bfloat16 [512], replicated, may hold values from 0.5 to 1.5
- kvb_weight: bfloat16 [512, 4096], P(None, 'narrow'), may hold values from -0.25 to 0.25
- o_weight: bfloat16 [2048, 2048], P('narrow'), may hold values from -0.125 to 0.125
- adapter_down: bfloat16 [2048, 1024], P(None, 'narrow'), may hold values from -0.125 to 0.125
- adapter_up_weight: bfloat16 [1024, 3072], P(None, 'narrow'), may hold values from -1.5 to 1.5
- lengths: int32 [64, 4], P('wide'), may hold values from 1 to 512, 1024 in all within a row
- adapter_ids: int32 [64, 4], P('wide'), may hold values from 0 to 63
- adapter_slot: int32 [64], replicated, may hold values from 0 to 63, each once
Outputs:
- hidden: bfloat16 [65536, 2048], P('wide', 'narrow')
- latent_cache: bfloat16 [65536, 576], P('wide')
Inputs may be any that keep to these rules, and one draw needn't show every extreme that they name: Each row of lengths sums to 1024, and its longest prompt is exactly 512.
All inputs are finite; a program needn't handle non-finite values.
Results may differ from a plain program's by a relative error of at most 0.0095.
The roundings to bfloat16 on the way count: a program that leaves them out, or rounds other values in their place, can miss the bound.
Values may be sent and summed in bfloat16 or wider, within the bound.
No kernel may reach another device: no remote copies, remote signals or barrier semaphores. Data moves between devices by JAX's collectives and lax.ppermute only.
A program may use at most 192 MiB of HBM per device.

v0:
```python
import jax
import jax.numpy as jnp
from jax import lax
from jax.sharding import PartitionSpec as P

NOPE = 128
ROPE = 64
VDIM = 128
LATENT = 512
RANK = 16
EPS = 1e-06
THETA = 50000.0
ADAPTER_SCALE = 2.0


def rms_scale(values, gain):
    mean_sq = jnp.mean(values * values, axis=-1, keepdims=True)
    return values * lax.rsqrt(mean_sq + EPS) * gain.astype(jnp.float32)


def rotate(values, positions):
    half = values.shape[-1] // 2
    freqs = jnp.exp(-jnp.log(THETA) * 2.0 * jnp.arange(half).astype(jnp.float32) / (2 * half))
    angle = positions.astype(jnp.float32)[:, None] * freqs[None, :]
    cosine = jnp.cos(angle)
    sine = jnp.sin(angle)
    if values.ndim == 3:
        cosine = cosine[:, None, :]
        sine = sine[:, None, :]
    first = values[..., :half]
    second = values[..., half:]
    return jnp.concatenate(
        [first * cosine - second * sine, first * sine + second * cosine], axis=-1
    )


def token_tables(length_row, id_row, adapter_slot, local_pos):
    ends = jnp.cumsum(length_row)
    starts = ends - length_row
    prompt = jnp.sum((ends[None, :] <= local_pos[:, None]).astype(jnp.int32), axis=1)
    onehot = (prompt[:, None] == jnp.arange(length_row.shape[0])[None, :]).astype(jnp.int32)
    position = local_pos - jnp.sum(onehot * starts[None, :], axis=1)
    adapter = jnp.sum(onehot * id_row[None, :], axis=1)
    slot_hot = (adapter[:, None] == jnp.arange(adapter_slot.shape[0])[None, :]).astype(jnp.int32)
    slot = jnp.sum(slot_hot * adapter_slot[None, :], axis=1)
    return (prompt, position, adapter, slot)


def pick_columns(stored, first_slots, prompts_here):
    blocks = [
        lax.dynamic_slice_in_dim(stored, first_slots[prompt_index] * RANK, RANK, 1)
        for prompt_index in range(prompts_here)
    ]
    return jnp.concatenate(blocks, axis=1)


def body(
    tokens,
    attn_gain,
    q_weight,
    kva_weight,
    kv_gain,
    kvb_weight,
    o_weight,
    adapter_down,
    adapter_up_weight,
    lengths,
    adapter_ids,
    adapter_slot,
):
    rows = tokens.shape[0]
    heads_here = o_weight.shape[0] // VDIM
    prompts_here = lengths.shape[1]
    whole = lax.all_gather(tokens, "narrow", axis=1, tiled=True)
    normed = rms_scale(whole.astype(jnp.float32), attn_gain).astype(jnp.bfloat16)
    local_pos = jnp.arange(rows)
    prompt, position, adapter, slot = token_tables(
        lengths[0], adapter_ids[0], adapter_slot, local_pos
    )
    query_vectors = jnp.dot(
        normed,
        lax.all_gather(q_weight, "wide", axis=0, tiled=True),
        preferred_element_type=jnp.float32,
    )
    kv_pre = jnp.dot(
        normed,
        lax.all_gather(kva_weight, "wide", axis=0, tiled=True),
        preferred_element_type=jnp.float32,
    )
    prompt_ids = adapter_ids[0]
    id_hot = (prompt_ids[:, None] == jnp.arange(adapter_slot.shape[0])[None, :]).astype(jnp.int32)
    prompt_position_slot = jnp.sum(id_hot * adapter_slot[None, :], axis=1)
    member = (prompt[:, None] == jnp.arange(prompts_here)[None, :]).astype(jnp.float32)
    stored = lax.all_gather(adapter_down, "narrow", axis=1, tiled=True)
    chosen = pick_columns(stored, prompt_position_slot, prompts_here)
    low = jnp.dot(normed, chosen, preferred_element_type=jnp.float32).reshape(
        rows, prompts_here, RANK
    )
    lowrank = jnp.sum(low * member[:, :, None], axis=1).astype(jnp.bfloat16)
    up_blocks = [
        lax.dynamic_slice_in_dim(adapter_up_weight, prompt_ids[prompt_index] * RANK, RANK, 0)
        for prompt_index in range(prompts_here)
    ]
    up_weight_rows = jnp.concatenate(up_blocks, axis=0)
    spread_rows = (member.astype(jnp.bfloat16)[:, :, None] * lowrank[:, None, :]).reshape(
        rows, prompts_here * RANK
    )
    query_vectors = query_vectors + ADAPTER_SCALE * jnp.dot(
        spread_rows, up_weight_rows, preferred_element_type=jnp.float32
    )
    query_vectors = query_vectors.reshape(rows, heads_here, NOPE + ROPE)
    query_vectors = jnp.concatenate(
        [query_vectors[..., :NOPE], rotate(query_vectors[..., NOPE:], position)], axis=-1
    ).astype(jnp.bfloat16)
    latent = rms_scale(kv_pre[:, :LATENT], kv_gain).astype(jnp.bfloat16)
    key_rope = rotate(kv_pre[:, LATENT:], position).astype(jnp.bfloat16)
    latent_cache = jnp.concatenate([latent, key_rope], axis=1)
    expanded = jnp.dot(latent, kvb_weight, preferred_element_type=jnp.float32).astype(jnp.bfloat16)
    expanded = expanded.reshape(rows, heads_here, NOPE + VDIM)
    key_nope = expanded[..., :NOPE]
    values = expanded[..., NOPE:]
    scale = 1.0 / jnp.sqrt(jnp.float32(NOPE + ROPE))
    scores = jnp.einsum(
        "qhd,khd->hqk", query_vectors[..., :NOPE], key_nope, preferred_element_type=jnp.float32
    )
    scores = scores + jnp.einsum(
        "qhd,kd->hqk", query_vectors[..., NOPE:], key_rope, preferred_element_type=jnp.float32
    )
    scores = scores * scale
    allowed = (prompt[None, :] == prompt[:, None]) & (local_pos[None, :] <= local_pos[:, None])
    scores = jnp.where(allowed[None, :, :], scores, jnp.float32(-1e30))
    top = jnp.max(scores, axis=-1, keepdims=True)
    expo = jnp.exp(scores - top)
    weights = (expo / jnp.sum(expo, axis=-1, keepdims=True)).astype(jnp.bfloat16)
    attended = jnp.einsum(
        "hqk,khd->qhd", weights, values, preferred_element_type=jnp.float32
    ).astype(jnp.bfloat16)
    attended = attended.reshape(rows, heads_here * VDIM)
    partial_out = jnp.dot(attended, o_weight, preferred_element_type=jnp.float32)
    projected = lax.psum_scatter(
        partial_out.astype(jnp.bfloat16), "narrow", scatter_dimension=1, tiled=True
    ).astype(jnp.float32)
    hidden = (tokens.astype(jnp.float32) + projected).astype(jnp.bfloat16)
    return (hidden, latent_cache)


def solution(mesh):
    return jax.shard_map(
        body,
        mesh=mesh,
        in_specs=(
            P("wide", "narrow"),
            P(),
            P("wide", "narrow"),
            P("wide", None),
            P(),
            P(None, "narrow"),
            P("narrow", None),
            P(None, "narrow"),
            P(None, "narrow"),
            P("wide", None),
            P("wide", None),
            P(),
        ),
        out_specs=(P("wide", "narrow"), P("wide", None)),
        check_vma=False,
    )
```

profile of v0, /device:TPU:1, one launch (start us, length us, event | category | flops | bytes accessed | tf_op | source)
XLA Modules:
  0.0 301.0 jit_solution(9721617435012271668)
XLA Ops:
  7.3 0.7 all-gather.5.cloned.1.call-update
  8.0 0.7 all-gather.11.cloned.1.call-update
  8.8 0.7 all-gather.7.cloned.1.call-update
  9.5 0.5 all-gather.9.cloned.1.call-update
  10.3 0.6 fusion.47
  13.5 0.7 fusion.46
  17.5 1.6 constant_dynamic-slice_fusion.3
  19.1 0.6 fusion.7
  19.7 10.1 %all-gather.5.cloned.1.call-done = bf16[1024,2048]{1,0:T(8,128)(2,1)} async-done(((bf16[1024,1024]{1,0:T(8,128)(2,1)}), bf16[1024,2048]{1,0:T(8,128)(2,1)}) %all-gather.5.cloned.1.call-update) | async-done | bytes 4194320 | tf_op jit(solution)/shard_map/all_gather | solution.py:74
  29.8 3.1 %fusion.4 = f32[1024]{0:T(1024)S(1)} fusion(bf16[1024,2048]{1,0:T(8,128)(2,1)} %all-gather.5.cloned.1.call-done), kind=kLoop, calls=%fused_computation.9 | loop fusion | flops 6290432 | bytes 4198400 | tf_op jit(solution)/shard_map/reduce_sum | solution.py:17
  32.9 16.3 %all-gather.11.cloned.1.call-done = bf16[2048,1024]{1,0:T(8,128)(2,1)} async-done(((bf16[2048,512]{1,0:T(8,128)(2,1)}), bf16[2048,1024]{1,0:T(8,128)(2,1)}) %all-gather.11.cloned.1.call-update) | async-done | bytes 4194320 | tf_op jit(solution)/shard_map/all_gather | solution.py:94
  49.2 2.4 constant_dynamic-slice_fusion.7
  52.0 2.0 fusion.17
  54.2 64.3 %all-gather.7.cloned.1.call-done = bf16[2048,576]{1,0:T(8,128)(2,1)} async-done(((bf16[32,576]{1,0:T(8,128)(2,1)}), bf16[2048,576]{1,0:T(8,128)(2,1)}) %all-gather.7.cloned.1.call-update) | async-done | bytes 2359312 | tf_op jit(solution)/shard_map/all_gather | solution.py:87
  118.5 5.7 %fusion.43 = f32[1024,576]{0,1:T(8,128)S(1)} fusion(bf16[2048,576]{1,0:T(8,128)(2,1)} %all-gather.7.cloned.1.call-done, bf16[1024,2048]{1,0:T(8,128)(2,1)} %all-gather.5.cloned.1.call-done, f32[2048]{0:T(1024)S(1)} %convert_element_type.88, f32[1024]{0:T(1024)S(1)} %add_rsqrt_fusion.1), kind=kOutput, calls=%fused_computation.81 | convolution fusion | flops 2424307712 | bytes 8925184 | tf_op jit(solution)/shard_map/dot_general | solution.py:85
  124.6 2.4 convolution_convert_fusion
  127.0 1.5 copy.40
  128.5 1.2 subtract_convert_fusion.1
  129.8 1.6 fusion.45
  131.4 60.1 %all-gather.9.cloned.1.call-done = bf16[2048,1536]{1,0:T(8,128)(2,1)} async-done(((bf16[32,1536]{1,0:T(8,128)(2,1)}), bf16[2048,1536]{1,0:T(8,128)(2,1)}) %all-gather.9.cloned.1.call-update) | async-done | bytes 6291472 | tf_op jit(solution)/shard_map/all_gather | solution.py:82
  191.4 10.1 %fusion.41 = f32[1024,1536]{1,0:T(8,128)S(1)} fusion(bf16[2048,1536]{1,0:T(8,128)(2,1)} %all-gather.9.cloned.1.call-done, bf16[1024,2048]{1,0:T(8,128)(2,1)} %all-gather.5.cloned.1.call-done, f32[2048]{0:T(1024)S(1)} %convert_element_type.88, f32[1024]{0:T(1024)S(1)} %add_rsqrt_fusion.1), kind=kOutput, calls=%fused_computation.80 | convolution fusion | flops 6450839552 | bytes 16789504 | tf_op jit(solution)/shard_map/dot_general | solution.py:80
  201.6 3.7 %multiply_add_fusion = f32[1024,1536]{1,0:T(8,128)} fusion(f32[1024,1536]{1,0:T(8,128)S(1)} %fusion.41, bf16[1024,64]{0,1:T(8,128)(2,1)S(1)} %bitcast.47, bf16[16,1536]{1,0:T(8,128)(2,1)S(1)} %copy-done.8, bf16[16,1536]{1,0:T(8,128)(2,1)S(1)} %copy-done.9, bf16[16,1536]{1,0:T(8,128)(2,1)S(1)} %copy-done.7, bf16[16,1536]{1,0:T(8,128)(2,1)S(1)} %copy-done.6), kind=kOutput, calls=%fused_computation.12 | convolution fusion | flops 205258752 | bytes 12910592 | tf_op jit(solution)/shard_map/dot_general | solution.py:108
  205.3 6.7 %copy.32 = f32[1024,1536]{0,1:T(8,128)} copy(f32[1024,1536]{1,0:T(8,128)} %multiply_add_fusion) | data formatting | bytes 12582912 | tf_op jit(solution)/shard_map/add | solution.py:108
  212.0 1.9 subtract_convert_fusion
  213.8 13.4 %fusion.13 = f32[1024,1024,8]{1,0,2:T(8,128)} fusion(bf16[1024,8,32]{0,2,1:T(8,128)(2,1)S(1)} %get-tuple-element.3, bf16[1024,8,32]{0,2,1:T(8,128)(2,1)S(1)} %get-tuple-element.2, bf16[1024,32]{0,1:T(8,128)(2,1)S(1)} %get-tuple-element.15, bf16[1024,32]{0,1:T(8,128)(2,1)S(1)} %get-tuple-element.14), kind=kOutput, calls=%fused_computation.25 | convolution fusion | flops 1076101120 | bytes 34734080 | tf_op jit(solution)/shard_map/qhd,kd->hqk/dot_general | solution.py:126
  227.2 26.8 %fusion.48 = (f32[8,1024]{1,0:T(8,128)S(1)}, f32[8,1024,1024]{1,2,0:T(8,128)}) fusion(f32[1024,1024,8]{1,0,2:T(8,128)} %fusion.13, pred[1024,1024]{0,1:T(8,128)(4,1)S(1)} %fusion.7, f32[1024,8,192]{0,2,1:T(8,128)} %bitcast.44, bf16[1024,8,128]{2,1,0:T(8,128)(2,1)S(1)} %get-tuple-element.5), kind=kOutput, calls=%fused_computation.85 | convolution fusion | flops 2189427712 | bytes 72384512 | tf_op jit(solution)/shard_map/sub | solution.py:133
  254.0 12.7 %fusion.10 = bf16[8,128,1024]{2,1,0:T(8,128)(2,1)S(1)} fusion(f32[8,1024,1024]{1,2,0:T(8,128)} %get-tuple-element.29, f32[8,1024]{1,0:T(8,128)S(1)} %get-tuple-element.28, bf16[1024,8,128]{2,1,0:T(8,128)(2,1)} %get-tuple-element.4), kind=kOutput, calls=%fused_computation.23 | convolution fusion | flops 2165309440 | bytes 37781504 | tf_op jit(solution)/shard_map/hqk,khd->qhd/dot_general | solution.py:135
  266.7 8.3 %convolution_convert_fusion.1 = bf16[1024,2048]{1,0:T(8,128)(2,1)} fusion(bf16[1024,1024]{0,1:T(8,128)(2,1)S(1)} %bitcast.52, bf16[1024,2048]{1,0:T(8,128)(2,1)} %param.18), kind=kOutput, calls=%fused_computation.18 | convolution fusion | flops 4297064448 | bytes 10485760 | tf_op jit(solution)/shard_map/dot_general | solution.py:139
  275.1 1.2 copy-done.4
  276.3 1.1 pad_maximum_fusion
  277.4 12.6 %reduce-scatter.2.cloned.1.call-done = bf16[1024,1024]{1,0:T(8,128)(2,1)} async-done(((bf16[1024,2048]{1,0:T(8,128)(2,1)}), bf16[1024,1024]{1,0:T(8,128)(2,1)}) %reduce-scatter.2.cloned.1.call-update) | async-done | bytes 2097168 | tf_op jit(solution)/shard_map/reduce_scatter | solution.py:140
  289.9 4.5 %add_convert_fusion = bf16[1024,1024]{1,0:T(8,128)(2,1)} fusion(bf16[1024,1024]{1,0:T(8,128)(2,1)} %reduce-scatter.2.cloned.1.call-done, bf16[1024,1024]{1,0:T(8,128)(2,1)} %param.12), kind=kLoop, calls=%fused_computation.14 | loop fusion | flops 4194304 | bytes 6291456 | tf_op jit(solution)/shard_map/convert_element_type | solution.py:143
  (53 shorter events, 2.3 us)
Async XLA Ops:
  7.2 117.4 %copy-start = (bf16[512,2048]{1,0:T(8,128)(2,1)S(1)}, bf16[512,2048]{1,0:T(8,128)(2,1)}, u32[]{:S(2)}) copy-start(bf16[512,2048]{1,0:T(8,128)(2,1)} %param.17) | copy-start | bytes 6291460
  7.2 2.9 copy-start.10
  7.2 2.9 copy-start.14
  7.2 9.3 %copy-start.15 = (s32[1,4]{1,0:T(1,128)S(1)}, s32[1,4]{1,0:T(1,128)}, u32[]{:S(2)}) copy-start(s32[1,4]{1,0:T(1,128)} %param.21) | copy-start | bytes 52
  7.2 9.5 %copy-start.12 = (bf16[512]{0:T(512)(128)(2,1)S(1)}, bf16[512]{0:T(512)(128)(2,1)}, u32[]{:S(2)}) copy-start(bf16[512]{0:T(512)(128)(2,1)} %param.16) | copy-start | bytes 3076
  7.2 9.5 %copy-start.11 = (bf16[2048]{0:T(1024)(128)(2,1)S(1)}, bf16[2048]{0:T(1024)(128)(2,1)}, u32[]{:S(2)}) copy-start(bf16[2048]{0:T(1024)(128)(2,1)} %param.13) | copy-start | bytes 12292
  7.2 22.5 %all-gather.5.cloned.1.call-start = ((), (), s32[]{:S(2)}) async-start(), calls=%async_computation.1 | async-start | bytes 6291456 | tf_op jit(solution)/shard_map/all_gather | solution.py:74
  8.0 41.2 %all-gather.11.cloned.1.call-start = ((), (), s32[]{:S(2)}) async-start(), calls=%async_computation.4 | async-start | bytes 6291456 | tf_op jit(solution)/shard_map/all_gather | solution.py:94
  8.7 109.8 %all-gather.7.cloned.1.call-start = ((), (), s32[]{:S(2)}) async-start(), calls=%async_computation.2 | async-start | bytes 2662400 | tf_op jit(solution)/shard_map/all_gather | solution.py:87
  9.5 182.0 %all-gather.9.cloned.1.call-start = ((), (), s32[]{:S(2)}) async-start(), calls=%async_computation.3 | async-start | bytes 6389760 | tf_op jit(solution)/shard_map/all_gather | solution.py:82
  10.0 279.9 %reduce-scatter.2.cloned.1.call-start = ((), (), s32[]{:S(2)}) async-start(), calls=%async_computation.5 | async-start | bytes 6291456 | tf_op jit(solution)/shard_map/reduce_scatter | solution.py:140
  49.2 2.9 copy-start.2
  124.6 2.4 copy-start.3
  127.0 1.5 copy-start.13
  191.4 10.2 %copy-start.6 = (bf16[16,1536]{1,0:T(8,128)(2,1)S(1)}, bf16[16,1536]{1,0:T(8,128)(2,1)}, u32[]{:S(2)}) copy-start(bf16[16,1536]{1,0:T(8,128)(2,1)} %get-tuple-element.10) | copy-start | bytes 147460
  191.4 10.2 %copy-start.7 = (bf16[16,1536]{1,0:T(8,128)(2,1)S(1)}, bf16[16,1536]{1,0:T(8,128)(2,1)}, u32[]{:S(2)}) copy-start(bf16[16,1536]{1,0:T(8,128)(2,1)} %get-tuple-element.11) | copy-start | bytes 147460
  191.4 10.2 %copy-start.8 = (bf16[16,1536]{1,0:T(8,128)(2,1)S(1)}, bf16[16,1536]{1,0:T(8,128)(2,1)}, u32[]{:S(2)}) copy-start(bf16[16,1536]{1,0:T(8,128)(2,1)} %get-tuple-element.12) | copy-start | bytes 147460
  191.4 10.2 %copy-start.9 = (bf16[16,1536]{1,0:T(8,128)(2,1)S(1)}, bf16[16,1536]{1,0:T(8,128)(2,1)}, u32[]{:S(2)}) copy-start(bf16[16,1536]{1,0:T(8,128)(2,1)} %get-tuple-element.13) | copy-start | bytes 147460
  205.3 6.7 %copy-start.5 = (f32[1024,32]{0,1:T(8,128)S(1)}, f32[1024,32]{0,1:T(8,128)}, u32[]{:S(2)}) copy-start(f32[1024,32]{0,1:T(8,128)} %get-tuple-element.17) | copy-start | bytes 393220
  275.0 1.2 copy-start.4
  276.3 18.2 %copy-start.1 = (bf16[512,2048]{1,0:T(8,128)(2,1)S(1)}, bf16[512,2048]{1,0:T(8,128)(2,1)}, u32[]{:S(2)}) copy-start(bf16[512,2048]{1,0:T(8,128)(2,1)} %param.17) | copy-start | bytes 6291460
Sparse Core Ops, SparseCore 0:
  9.7 20.0 all-gather.4
  31.4 17.6 all-gather.10
  52.1 66.3 all-gather.6
  121.1 70.3 all-gather.8
  275.2 14.6 reduce-scatter.1
where the time goes:
time: 301 us
  waiting for transfers between devices  166 us (55%)
  matrix products  85.1 us (28%)
  between operations  19.1 us (6%)
  local copies, waits for them, and re-layouts  16.7 us (6%)
  other arithmetic  13.9 us (5%)
    all_gather x1, waiting for transfers between devices, body(): lax.all_gather(kva_weight, 'wide', axis=0, tiled=True)  64.3 us
    all_gather x1, waiting for transfers between devices, body(): lax.all_gather(q_weight, 'wide', axis=0, tiled=True)  60.1 us
    sub x1, matrix products, body(): expo = jnp.exp(scores - top)  26.8 us
    all_gather x1, waiting for transfers between devices, body(): stored = lax.all_gather(adapter_down, 'narrow', axis=1, tiled=True)  16.3 us
    dot_general x1, matrix products, body(): jnp.einsum('qhd,kd->hqk', query_vectors[..., NOPE:], key_rope, preferred_...  13.4 us
    dot_general x1, matrix products, body(): jnp.einsum('hqk,khd->qhd', weights, values, preferred_element_type=jnp.fl...  12.7 us
    reduce_scatter x1, waiting for transfers between devices, body(): lax.psum_scatter(partial_out.astype(jnp.bfloat16), 'narrow', scatter_dime...  12.6 us
    dot_general x1, matrix products, body(): jnp.dot(normed, lax.all_gather(q_weight, 'wide', axis=0, tiled=True), pre...  10.1 us
  transfers between devices with their start and end apart: 5, of which 5 were waited for; matrix products, arithmetic and copies ran while one was open for 9% of the time, Pallas kernels for 0%

commit v1 on v0

--- a/solution.py
+++ b/solution.py
@@ -1,3 +1,4 @@
+import functools
 import jax
 import jax.numpy as jnp
 from jax import lax
@@ -11,6 +12,16 @@
 EPS = 1e-06
 THETA = 50000.0
 ADAPTER_SCALE = 2.0
+
+
+def assign_tokens(work_x, at_axis):
+    x_next = jnp.concatenate(tuple((work_x for _ in range(lax.axis_size("wide")))), axis=at_axis)
+    return lax.all_to_all(
+        x_next, concat_axis=at_axis, axis_name="wide", tiled=True, split_axis=at_axis
+    )
+
+
+see_routes_all = functools.partial(assign_tokens, at_axis=0)
 
 
 def rms_scale(values, gain):
@@ -82,11 +93,7 @@
         lax.all_gather(q_weight, "wide", axis=0, tiled=True),
         preferred_element_type=jnp.float32,
     )
-    kv_pre = jnp.dot(
-        normed,
-        lax.all_gather(kva_weight, "wide", axis=0, tiled=True),
-        preferred_element_type=jnp.float32,
-    )
+    kv_pre = jnp.dot(normed, see_routes_all(kva_weight), preferred_element_type=jnp.float32)
     prompt_ids = adapter_ids[0]
     id_hot = (prompt_ids[:, None] == jnp.arange(adapter_slot.shape[0])[None, :]).astype(jnp.int32)
     prompt_position_slot = jnp.sum(id_hot * adapter_slot[None, :], axis=1)

time: 301 us -> 235 us (0.78)
  waiting for transfers between devices: 166 us -> 80.2 us
  starting transfers between devices: 0.19 us -> 12.5 us
  local copies, waits for them, and re-layouts: 16.7 us -> 21.9 us
    all_gather x1 -> x0, waiting for transfers between devices: 64.3 us -> none  [body(): lax.all_gather(kva_weight, 'wide', axis=0, tiled=True)]
    all_to_all x0 -> x1, waiting for transfers between devices: none -> 20.6 us  [assign_tokens(): lax.all_to_all(x_next, concat_axis=at_axis, axis_name='wide', tiled=True,...]
    all_gather x1, waiting for transfers between devices: 16.3 us -> 0.01 us  [body(): stored = lax.all_gather(adapter_down, 'narrow', axis=1, tiled=True)]
    all_gather x1, waiting for transfers between devices: 60.1 us -> 44.9 us  [body(): lax.all_gather(q_weight, 'wide', axis=0, tiled=True)]
    all_to_all x0 -> x1, starting transfers between devices: none -> 12.3 us  [assign_tokens(): lax.all_to_all(x_next, concat_axis=at_axis, axis_name='wide', tiled=True,...]
    all_gather x1, waiting for transfers between devices: 10.1 us -> 0.02 us  [body(): whole = lax.all_gather(tokens, 'narrow', axis=1, tiled=True)]
    unnamed x33 -> x104, local copies, waits for them, and re-layouts: 3.27 us -> 8.41 us
  transfers between devices with their start and end apart: 5 -> 5, of which waited for: 5 -> 3; matrix products, arithmetic and copies ran while one was open for 9% -> 13% of each run, Pallas kernels for 0% -> 0%
where the time goes in v1:
time: 235 us; the launch traced here: 234 us
  matrix products  85.1 us (36%)
  waiting for transfers between devices  80.2 us (34%)
  local copies, waits for them, and re-layouts  21.9 us (9%)
  between operations  19.5 us (8%)
  other arithmetic  14.8 us (6%)
  starting transfers between devices  12.5 us (5%)
    all_gather x1, waiting for transfers between devices, body(): lax.all_gather(q_weight, 'wide', axis=0, tiled=True)  44.9 us
    sub x1, matrix products, body(): expo = jnp.exp(scores - top)  26.8 us
    all_to_all x1, waiting for transfers between devices, assign_tokens(): lax.all_to_all(x_next, concat_axis=at_axis, axis_name='wide', tiled=True,...  20.6 us
    dot_general x1, matrix products, body(): jnp.einsum('qhd,kd->hqk', query_vectors[..., NOPE:], key_rope, preferred_...  13.2 us
    dot_general x1, matrix products, body(): jnp.einsum('hqk,khd->qhd', weights, values, preferred_element_type=jnp.fl...  12.7 us
    reduce_scatter x1, waiting for transfers between devices, body(): lax.psum_scatter(partial_out.astype(jnp.bfloat16), 'narrow', scatter_dime...  12.5 us
    all_to_all x1, starting transfers between devices, assign_tokens(): lax.all_to_all(x_next, concat_axis=at_axis, axis_name='wide', tiled=True,...  12.3 us
    dot_general x1, matrix products, body(): jnp.dot(normed, lax.all_gather(q_weight, 'wide', axis=0, tiled=True), pre...  10.4 us
  transfers between devices with their start and end apart: 5, of which 3 were waited for; matrix products, arithmetic and copies ran while one was open for 13% of the time, Pallas kernels for 0%

profile of v1, /device:TPU:1, one launch (start us, length us, event | category | flops | bytes accessed | tf_op | source)
XLA Modules:
  0.0 234.1 jit_solution(6093972369936686567)
XLA Ops:
  7.2 0.7 all-gather.4.cloned.1.call-update
  8.0 0.7 all-gather.8.cloned.1.call-update
  8.7 0.7 all-gather.6.cloned.1.call-update
  10.4 1.5 copy-done.8
  11.9 12.3 %all-to-all-start = ((bf16[64,32,576]{2,1,0:T(8,128)(2,1)}), bf16[64,32,576]{2,1,0:T(8,128)(2,1)}, u32[]{:S(2)}, u32[]{:S(2)}) async-start(bf16[64,32,576]{2,1,0:T(8,128)(2,1)} %bitcast.49), calls=%async_computation | async-start | bytes 5242880 | tf_op jit(solution)/shard_map/all_to_all | solution.py:19
  24.5 0.7 fusion.47
  27.8 0.7 fusion.46
  32.1 1.6 constant_dynamic-slice_fusion.3
  33.7 0.6 fusion.7
  34.3 3.1 %fusion.4 = f32[1024]{0:T(1024)S(1)} fusion(bf16[1024,2048]{1,0:T(8,128)(2,1)} %all-gather.4.cloned.1.call-done), kind=kLoop, calls=%fused_computation.9 | loop fusion | flops 6290432 | bytes 4198400 | tf_op jit(solution)/shard_map/reduce_sum | solution.py:28
  37.4 20.6 %all-to-all-done = bf16[64,32,576]{2,1,0:T(8,128)(2,1)} async-done(((bf16[64,32,576]{2,1,0:T(8,128)(2,1)}), bf16[64,32,576]{2,1,0:T(8,128)(2,1)}, u32[]{:S(2)}, u32[]{:S(2)}) %all-to-all-start) | async-done | bytes 2359328 | tf_op jit(solution)/shard_map/all_to_all | solution.py:19
  58.0 5.7 %fusion.43 = f32[1024,576]{0,1:T(8,128)S(1)} fusion(bf16[2048,576]{1,0:T(8,128)(2,1)} %bitcast.1, bf16[1024,2048]{1,0:T(8,128)(2,1)} %all-gather.4.cloned.1.call-done, f32[2048]{0:T(1024)S(1)} %convert_element_type.88, f32[1024]{0:T(1024)S(1)} %add_rsqrt_fusion.1), kind=kOutput, calls=%fused_computation.145 | convolution fusion | flops 2424307712 | bytes 8925184 | tf_op jit(solution)/shard_map/dot_general | solution.py:96
  64.2 0.9 copy-done.4
  65.1 2.4 %convolution_convert_fusion = bf16[1024,2048]{1,0:T(8,128)(2,1)S(1)} fusion(bf16[1024,512]{0,1:T(8,128)(2,1)S(1)} %multiply_convert_fusion, bf16[512,2048]{1,0:T(8,128)(2,1)S(1)} %copy-done), kind=kOutput, calls=%fused_computation.17 | convolution fusion | flops 2149580800 | bytes 7340032 | tf_op jit(solution)/shard_map/dot_general | solution.py:125
  67.5 3.4 %copy.40 = bf16[128,8,8,256]{3,2,1,0:T(8,128)(2,1)} copy(bf16[128,8,8,256]{3,1,2,0:T(8,128)(2,1)S(1)} %bitcast.48) | data formatting | bytes 8388608
  70.9 2.4 %constant_dynamic-slice_fusion.7 = (bf16[2048,16]{1,0:T(8,128)(2,1)S(1)}, bf16[2048,16]{1,0:T(8,128)(2,1)S(1)}, bf16[2048,16]{1,0:T(8,128)(2,1)S(1)}, bf16[2048,16]{1,0:T(8,128)(2,1)S(1)}) fusion(bf16[2048,1024]{1,0:T(8,128)(2,1)} %all-gather.8.cloned.1.call-done, s32[]{:T(128)S(6)} %select_n.28, s32[]{:T(128)S(6)} %select_n.31, s32[]{:T(128)S(6)} %select_n.30, ...), kind=kLoop, calls=%fused_computation.137 | loop fusion | bytes 524304 | tf_op jit(solution)/shard_map/dynamic_slice | solution.py:62
  73.9 2.0 fusion.17
  76.0 2.2 subtract_convert_fusion.1
  78.1 1.6 fusion.45
  79.7 44.9 %all-gather.6.cloned.1.call-done = bf16[2048,1536]{1,0:T(8,128)(2,1)} async-done(((bf16[32,1536]{1,0:T(8,128)(2,1)}), bf16[2048,1536]{1,0:T(8,128)(2,1)}) %all-gather.6.cloned.1.call-update) | async-done | bytes 6291472 | tf_op jit(solution)/shard_map/all_gather | solution.py:93
  124.7 10.4 %fusion.41 = f32[1024,1536]{1,0:T(8,128)S(1)} fusion(bf16[2048,1536]{1,0:T(8,128)(2,1)} %all-gather.6.cloned.1.call-done, bf16[1024,2048]{1,0:T(8,128)(2,1)} %all-gather.4.cloned.1.call-done, f32[2048]{0:T(1024)S(1)} %convert_element_type.88, f32[1024]{0:T(1024)S(1)} %add_rsqrt_fusion.1), kind=kOutput, calls=%fused_computation.144 | convolution fusion | flops 6450839552 | bytes 16789504 | tf_op jit(solution)/shard_map/dot_general | solution.py:91
  135.1 3.7 %multiply_add_fusion = f32[1024,1536]{1,0:T(8,128)} fusion(f32[1024,1536]{1,0:T(8,128)S(1)} %fusion.41, bf16[1024,64]{0,1:T(8,128)(2,1)S(1)} %bitcast.50, bf16[16,1536]{1,0:T(8,128)(2,1)S(1)} %copy-done.12, bf16[16,1536]{1,0:T(8,128)(2,1)S(1)} %copy-done.13, bf16[16,1536]{1,0:T(8,128)(2,1)S(1)} %copy-done.11, bf16[16,1536]{1,0:T(8,128)(2,1)S(1)} %copy-done.10), kind=kOutput, calls=%fused_computation.12 | convolution fusion | flops 205258752 | bytes 12910592 | tf_op jit(solution)/shard_map/dot_general | solution.py:115
  138.8 6.6 %copy.32 = f32[1024,1536]{0,1:T(8,128)} copy(f32[1024,1536]{1,0:T(8,128)} %multiply_add_fusion) | data formatting | bytes 12582912 | tf_op jit(solution)/shard_map/add | solution.py:115
  145.4 1.9 subtract_convert_fusion
  147.3 13.2 %fusion.13 = f32[1024,1024,8]{1,0,2:T(8,128)} fusion(bf16[1024,8,32]{0,2,1:T(8,128)(2,1)S(1)} %get-tuple-element.3, bf16[1024,8,32]{0,2,1:T(8,128)(2,1)S(1)} %get-tuple-element.2, bf16[1024,32]{0,1:T(8,128)(2,1)S(1)} %get-tuple-element.15, bf16[1024,32]{0,1:T(8,128)(2,1)S(1)} %get-tuple-element.14), kind=kOutput, calls=%fused_computation.25 | convolution fusion | flops 1076101120 | bytes 34734080 | tf_op jit(solution)/shard_map/qhd,kd->hqk/dot_general | solution.py:133
  160.5 26.8 %fusion.48 = (f32[8,1024]{1,0:T(8,128)S(1)}, f32[8,1024,1024]{1,2,0:T(8,128)}) fusion(f32[1024,1024,8]{1,0,2:T(8,128)} %fusion.13, pred[1024,1024]{0,1:T(8,128)(4,1)S(1)} %fusion.7, f32[1024,8,192]{0,2,1:T(8,128)} %bitcast.46, bf16[1024,8,128]{2,1,0:T(8,128)(2,1)S(1)} %get-tuple-element.5), kind=kOutput, calls=%fused_computation.149 | convolution fusion | flops 2189427712 | bytes 72384512 | tf_op jit(solution)/shard_map/sub | solution.py:140
  187.2 12.7 %fusion.10 = bf16[8,128,1024]{2,1,0:T(8,128)(2,1)S(1)} fusion(f32[8,1024,1024]{1,2,0:T(8,128)} %get-tuple-element.29, f32[8,1024]{1,0:T(8,128)S(1)} %get-tuple-element.28, bf16[1024,8,128]{2,1,0:T(8,128)(2,1)} %get-tuple-element.4), kind=kOutput, calls=%fused_computation.23 | convolution fusion | flops 2165309440 | bytes 37781504 | tf_op jit(solution)/shard_map/hqk,khd->qhd/dot_general | solution.py:142
  199.9 8.3 %convolution_convert_fusion.1 = bf16[1024,2048]{1,0:T(8,128)(2,1)} fusion(bf16[1024,1024]{0,1:T(8,128)(2,1)S(1)} %bitcast.55, bf16[1024,2048]{1,0:T(8,128)(2,1)} %param.18), kind=kOutput, calls=%fused_computation.18 | convolution fusion | flops 4297064448 | bytes 10485760 | tf_op jit(solution)/shard_map/dot_general | solution.py:146
  208.3 1.2 copy-done.7
  209.5 1.1 pad_maximum_fusion
  210.6 12.5 %reduce-scatter.2.cloned.1.call-done = bf16[1024,1024]{1,0:T(8,128)(2,1)} async-done(((bf16[1024,2048]{1,0:T(8,128)(2,1)}), bf16[1024,1024]{1,0:T(8,128)(2,1)}) %reduce-scatter.2.cloned.1.call-update) | async-done | bytes 2097168 | tf_op jit(solution)/shard_map/reduce_scatter | solution.py:147
  223.1 4.5 %add_convert_fusion = bf16[1024,1024]{1,0:T(8,128)(2,1)} fusion(bf16[1024,1024]{1,0:T(8,128)(2,1)} %reduce-scatter.2.cloned.1.call-done, bf16[1024,1024]{1,0:T(8,128)(2,1)} %param.12), kind=kLoop, calls=%fused_computation.14 | loop fusion | flops 4194304 | bytes 6291456 | tf_op jit(solution)/shard_map/convert_element_type | solution.py:150
  (124 shorter events, 3.1 us)
Async XLA Ops:
  7.2 57.9 %copy-start = (bf16[512,2048]{1,0:T(8,128)(2,1)S(1)}, bf16[512,2048]{1,0:T(8,128)(2,1)}, u32[]{:S(2)}) copy-start(bf16[512,2048]{1,0:T(8,128)(2,1)} %param.17) | copy-start | bytes 6291460
  7.2 2.2 copy-start.2
  7.2 27.1 %all-gather.4.cloned.1.call-start = ((), (), s32[]{:S(2)}) async-start(), calls=%async_computation.2 | async-start | bytes 6291456 | tf_op jit(solution)/shard_map/all_gather | solution.py:85
  7.9 63.0 %all-gather.8.cloned.1.call-start = ((), (), s32[]{:S(2)}) async-start(), calls=%async_computation.4 | async-start | bytes 6291456 | tf_op jit(solution)/shard_map/all_gather | solution.py:101
  8.7 116.0 %all-gather.6.cloned.1.call-start = ((), (), s32[]{:S(2)}) async-start(), calls=%async_computation.3 | async-start | bytes 6389760 | tf_op jit(solution)/shard_map/all_gather | solution.py:93
  10.4 1.5 copy-start.8
  11.9 12.4 %copy-start.14 = (s32[1,4]{1,0:T(1,128)S(1)}, s32[1,4]{1,0:T(1,128)}, u32[]{:S(2)}) copy-start(s32[1,4]{1,0:T(1,128)} %param.22) | copy-start | bytes 52
  11.9 12.4 %copy-start.18 = (s32[64]{0:T(128)S(1)}, s32[64]{0:T(128)}, u32[]{:S(2)}) copy-start(s32[64]{0:T(128)} %param.23) | copy-start | bytes 772
  11.9 19.2 %copy-start.19 = (s32[1,4]{1,0:T(1,128)S(1)}, s32[1,4]{1,0:T(1,128)}, u32[]{:S(2)}) copy-start(s32[1,4]{1,0:T(1,128)} %param.21) | copy-start | bytes 52
  11.9 19.4 %copy-start.16 = (bf16[512]{0:T(512)(128)(2,1)S(1)}, bf16[512]{0:T(512)(128)(2,1)}, u32[]{:S(2)}) copy-start(bf16[512]{0:T(512)(128)(2,1)} %param.16) | copy-start | bytes 3076
  11.9 19.4 %copy-start.15 = (bf16[2048]{0:T(1024)(128)(2,1)S(1)}, bf16[2048]{0:T(1024)(128)(2,1)}, u32[]{:S(2)}) copy-start(bf16[2048]{0:T(1024)(128)(2,1)} %param.13) | copy-start | bytes 12292
  11.9 46.1 %all-to-all-start = ((bf16[64,32,576]{2,1,0:T(8,128)(2,1)}), bf16[64,32,576]{2,1,0:T(8,128)(2,1)}, u32[]{:S(2)}, u32[]{:S(2)}) async-start(bf16[64,32,576]{2,1,0:T(8,128)(2,1)} %bitcast.49), calls=%async_computation | async-start | bytes 5242880 | tf_op jit(solution)/shard_map/all_to_all | solution.py:19
  24.3 198.8 %reduce-scatter.2.cloned.1.call-start = ((), (), s32[]{:S(2)}) async-start(), calls=%async_computation.5 | async-start | bytes 6291456 | tf_op jit(solution)/shard_map/reduce_scatter | solution.py:147
  63.7 1.4 copy-start.4
  65.1 2.4 %copy-start.6 = (bf16[1024,512]{0,1:T(8,128)(2,1)}, bf16[1024,512]{0,1:T(8,128)(2,1)S(1)}, u32[]{:S(2)}) copy-start(bf16[1024,512]{0,1:T(8,128)(2,1)S(1)} %multiply_convert_fusion) | copy-start | bytes 3145732
  70.9 2.9 %copy-start.5 = (bf16[1024,2048]{1,0:T(8,128)(2,1)S(1)}, bf16[1024,2048]{1,0:T(8,128)(2,1)}, u32[]{:S(2)}) copy-start(bf16[1024,2048]{1,0:T(8,128)(2,1)} %all-gather.4.cloned.1.call-done) | copy-start | bytes 12582916
  73.8 2.1 copy-start.17
  73.9 4.3 %copy-start.3 = (bf16[128,8,8,256]{3,2,1,0:T(8,128)(2,1)S(1)}, bf16[128,8,8,256]{3,2,1,0:T(8,128)(2,1)}, u32[]{:S(2)}) copy-start(bf16[128,8,8,256]{3,2,1,0:T(8,128)(2,1)} %copy.40) | copy-start | bytes 12582916
  124.7 10.4 %copy-start.10 = (bf16[16,1536]{1,0:T(8,128)(2,1)S(1)}, bf16[16,1536]{1,0:T(8,128)(2,1)}, u32[]{:S(2)}) copy-start(bf16[16,1536]{1,0:T(8,128)(2,1)} %get-tuple-element.10) | copy-start | bytes 147460
  124.7 10.4 %copy-start.11 = (bf16[16,1536]{1,0:T(8,128)(2,1)S(1)}, bf16[16,1536]{1,0:T(8,128)(2,1)}, u32[]{:S(2)}) copy-start(bf16[16,1536]{1,0:T(8,128)(2,1)} %get-tuple-element.11) | copy-start | bytes 147460
  124.7 10.4 %copy-start.12 = (bf16[16,1536]{1,0:T(8,128)(2,1)S(1)}, bf16[16,1536]{1,0:T(8,128)(2,1)}, u32[]{:S(2)}) copy-start(bf16[16,1536]{1,0:T(8,128)(2,1)} %get-tuple-element.12) | copy-start | bytes 147460
  124.7 10.4 %copy-start.13 = (bf16[16,1536]{1,0:T(8,128)(2,1)S(1)}, bf16[16,1536]{1,0:T(8,128)(2,1)}, u32[]{:S(2)}) copy-start(bf16[16,1536]{1,0:T(8,128)(2,1)} %get-tuple-element.13) | copy-start | bytes 147460
  138.8 6.7 %copy-start.9 = (f32[1024,32]{0,1:T(8,128)S(1)}, f32[1024,32]{0,1:T(8,128)}, u32[]{:S(2)}) copy-start(f32[1024,32]{0,1:T(8,128)} %get-tuple-element.17) | copy-start | bytes 393220
  208.3 1.2 copy-start.7
  209.5 18.1 %copy-start.1 = (bf16[512,2048]{1,0:T(8,128)(2,1)S(1)}, bf16[512,2048]{1,0:T(8,128)(2,1)}, u32[]{:S(2)}) copy-start(bf16[512,2048]{1,0:T(8,128)(2,1)} %param.17) | copy-start | bytes 6291460
Sparse Core Ops, SparseCore 0:
  9.7 20.0 all-gather.3
  31.4 17.6 all-gather.7
  51.9 72.7 all-gather.5
  208.4 14.6 reduce-scatter.1
